TPU v7x, 32 devices: a whole 2x2x4 slice. The times are simulated.
32 devices in a mesh: grp: 4 (over x, core), ep: 8 (over z, y).
Axes of the slice: x: 2, y: 2, z: 4, core: 2. Of those that a mesh axis runs over, the one named last changes fastest.
Arguments:
- tokens: bfloat16 [2048, 5120], P('ep', 'grp'), may hold values from -6 to 6
- cotangent: bfloat16 [2048, 5120], P('ep', 'grp'), may hold values from -0.59765625 to 0.59765625
- gate_weights: bfloat16 [2048, 6], P('ep'), may hold values from 0.099609375 to 1
- expert_ids: int32 [2048, 6], P('ep'), may hold values from 0 to 159, all different within a row; in each aligned block of 256 rows (0 to 255, 256 to 511, ...) at most 16 rows name the same one
- hot_ids: int32 [2], replicated, may hold values from 8 to 159, as said below
- gate_cold: bfloat16 [8, 5120, 768], P('ep', 'grp'), may hold values from -0.078125 to 0.078125
- up_cold: bfloat16 [8, 5120, 768], P('ep', 'grp'), may hold values from -0.078125 to 0.078125
- down_cold: bfloat16 [8, 768, 5120], P('ep', None, 'grp'), may hold values from -0.21875 to 0.21875
- gate_hot: bfloat16 [2, 5120, 768], P(None, 'grp', 'ep'), may hold values from -0.078125 to 0.078125
- up_hot: bfloat16 [2, 5120, 768], P(None, 'grp', 'ep'), may hold values from -0.078125 to 0.078125
- down_hot: bfloat16 [2, 768, 5120], P(None, 'ep', 'grp'), may hold values from -0.21875 to 0.21875
Outputs:
- grad_gate_cold: bfloat16 [8, 5120, 768], P('ep', 'grp')
- grad_up_cold: bfloat16 [8, 5120, 768], P('ep', 'grp')
- grad_down_cold: bfloat16 [8, 768, 5120], P('ep', None, 'grp')
- grad_gate_hot: float32 [2, 5120, 768], P(None, 'grp', 'ep')
- grad_up_hot: float32 [2, 5120, 768], P(None, 'grp', 'ep')
- grad_down_hot: float32 [2, 768, 5120], P(None, 'ep', 'grp')
- gate_weight_grad: float32 [2048, 6], P('ep')
Inputs may be any that keep to these rules, and one draw needn't show every extreme that they name: `expert_ids`: each row names 6 different experts. Among the routes of the 256 tokens of one index of ep (aligned blocks of rows) no expert is named more than 16 times, a bound that some block reaches. `hot_ids`: distinct expert numbers, none below 8; expert 160 - 1 is always among them.
All inputs are finite; a program needn't handle non-finite values.
Results may differ from a plain program's by a relative error of at most 0.02.
Values may be sent and summed in bfloat16 or wider, within the bound.
No kernel may reach another device: no remote copies, remote signals or barrier semaphores. Data moves between devices by JAX's collectives and lax.ppermute only.
A program may use at most 128 MiB of HBM per device.

v0:
```python
import jax
import jax.numpy as jnp
from jax import lax
from jax.sharding import PartitionSpec as P


def route_table(flat_ids, targets, capacity):
    matches = (flat_ids[:, None] == targets[None, :]).astype(jnp.int32)
    rank_of = jnp.cumsum(matches, axis=0) - 1
    slot_of = jnp.sum(matches * rank_of, axis=1)
    owner_of = jnp.sum(matches * jnp.arange(targets.shape[0], dtype=jnp.int32)[None, :], axis=1)
    usable = jnp.sum(matches, axis=1) > 0
    row_of = owner_of * capacity + slot_of
    rows_total = targets.shape[0] * capacity
    route_map = (row_of[None, :] == jnp.arange(rows_total, dtype=jnp.int32)[:, None]) & usable[
        None, :
    ]
    return route_map.astype(jnp.float32)


def gather_rows(route_map, tokens, cotangent, flat_weights, tok_rows, top_count):
    per_token = jnp.sum(route_map.reshape(route_map.shape[0], tok_rows, top_count), axis=2)
    token_map = per_token.astype(jnp.bfloat16)
    feat_rows = jnp.dot(token_map, tokens, preferred_element_type=jnp.float32).astype(jnp.bfloat16)
    cotan_rows = jnp.dot(token_map, cotangent, preferred_element_type=jnp.float32).astype(
        jnp.bfloat16
    )
    scale_rows = jnp.dot(
        route_map, flat_weights.astype(jnp.float32), precision=lax.Precision.HIGHEST
    )
    return (feat_rows, cotan_rows, scale_rows.astype(jnp.bfloat16))


def swiglu_back(pre_gate, pre_up, grad_hidden):
    sigmoid_gate = jax.nn.sigmoid(pre_gate)
    activated = pre_gate * sigmoid_gate
    hidden = (activated * pre_up).astype(jnp.bfloat16)
    back_gate = (
        grad_hidden * pre_up * sigmoid_gate * (1.0 + pre_gate * (1.0 - sigmoid_gate))
    ).astype(jnp.bfloat16)
    back_up = (grad_hidden * activated).astype(jnp.bfloat16)
    return (hidden, back_gate, back_up)


def body(
    tokens,
    cotangent,
    gate_weights,
    expert_ids,
    hot_ids,
    gate_cold,
    up_cold,
    down_cold,
    gate_hot,
    up_hot,
    down_hot,
):
    tok_rows, slice_width = tokens.shape
    top_count = expert_ids.shape[1]
    cold_count = lax.axis_size("ep")
    hot_count = hot_ids.shape[0]
    capacity = tok_rows // 16
    flat_ids = expert_ids.reshape(-1)
    flat_weights = gate_weights.reshape(-1)
    cold_map = route_table(flat_ids, jnp.arange(cold_count, dtype=jnp.int32), capacity)
    hot_map = route_table(flat_ids, hot_ids, capacity)
    cold_feats, cold_cotan, cold_scale = gather_rows(
        cold_map, tokens, cotangent, flat_weights, tok_rows, top_count
    )
    hot_feats, hot_cotan, hot_scale = gather_rows(
        hot_map, tokens, cotangent, flat_weights, tok_rows, top_count
    )
    outgoing = (
        cold_feats.reshape(cold_count, capacity, slice_width),
        cold_cotan.reshape(cold_count, capacity, slice_width),
        cold_scale.reshape(cold_count, capacity),
    )
    recv_feats, recv_cotan, recv_scale = (
        lax.all_to_all(outgoing[0], "ep", split_axis=0, concat_axis=0, tiled=True),
        lax.all_to_all(outgoing[1], "ep", split_axis=0, concat_axis=0, tiled=True),
        lax.all_to_all(outgoing[2], "ep", split_axis=0, concat_axis=0, tiled=True),
    )
    recv_feats = recv_feats.reshape(-1, slice_width)
    recv_cotan = recv_cotan.reshape(-1, slice_width)
    weighted = (
        recv_scale.reshape(-1).astype(jnp.float32)[:, None] * recv_cotan.astype(jnp.float32)
    ).astype(jnp.bfloat16)
    w_gate = gate_cold[0]
    w_up = up_cold[0]
    w_down = down_cold[0]
    part_gate = jnp.dot(recv_feats, w_gate, preferred_element_type=jnp.float32)
    part_up = jnp.dot(recv_feats, w_up, preferred_element_type=jnp.float32)
    part_hidden = lax.dot_general(
        weighted, w_down, (((1,), (1,)), ((), ())), preferred_element_type=jnp.float32
    )
    pre_gate, pre_up, grad_hidden = (
        lax.psum(part_gate.astype(jnp.bfloat16), "grp").astype(jnp.float32),
        lax.psum(part_up.astype(jnp.bfloat16), "grp").astype(jnp.float32),
        lax.psum(part_hidden.astype(jnp.bfloat16), "grp").astype(jnp.float32),
    )
    hidden, back_gate, back_up = swiglu_back(pre_gate, pre_up, grad_hidden)
    output_slice = jnp.dot(hidden, w_down, preferred_element_type=jnp.float32)
    cold_route = jnp.sum(output_slice * recv_cotan.astype(jnp.float32), axis=1)
    contract_rows = (((0,), (0,)), ((), ()))
    grad_gate_cold = lax.dot_general(
        recv_feats, back_gate, contract_rows, preferred_element_type=jnp.float32
    )
    grad_up_cold = lax.dot_general(
        recv_feats, back_up, contract_rows, preferred_element_type=jnp.float32
    )
    grad_down_cold = lax.dot_general(
        hidden, weighted, contract_rows, preferred_element_type=jnp.float32
    )
    hot_weighted_local = (
        hot_scale.astype(jnp.float32)[:, None] * hot_cotan.astype(jnp.float32)
    ).astype(jnp.bfloat16)
    blocks = lax.axis_size("ep")
    stacked = jnp.stack([hot_feats, hot_cotan, hot_weighted_local])
    all_rows = lax.all_gather(stacked, "ep", axis=1, tiled=False)
    all_rows = all_rows.reshape(3, blocks, hot_count, capacity, slice_width)
    all_rows = jnp.transpose(all_rows, (0, 2, 1, 3, 4)).reshape(
        3, hot_count, blocks * capacity, slice_width
    )
    rows_feat, rows_cot, rows_wt = (all_rows[0], all_rows[1], all_rows[2])
    part_gate_hot = jnp.einsum(
        "jrd,jdh->jrh", rows_feat, gate_hot, preferred_element_type=jnp.float32
    )
    part_up_hot = jnp.einsum("jrd,jdh->jrh", rows_feat, up_hot, preferred_element_type=jnp.float32)
    part_hidden_hot = jnp.einsum(
        "jrd,jhd->jrh", rows_wt, down_hot, preferred_element_type=jnp.float32
    )
    cot_down = jnp.einsum("jrd,jhd->jrh", rows_cot, down_hot, preferred_element_type=jnp.float32)
    hot_parts = lax.psum(
        jnp.stack([part_gate_hot, part_up_hot, part_hidden_hot]).astype(jnp.bfloat16), "grp"
    ).astype(jnp.float32)
    hidden_hot, back_gate_hot, back_up_hot = swiglu_back(hot_parts[0], hot_parts[1], hot_parts[2])
    hot_route_part = jnp.sum(hidden_hot.astype(jnp.float32) * cot_down, axis=2)
    hidden_blk = hidden_hot.shape[2]
    feat_b = rows_feat.reshape(hot_count, blocks, capacity, slice_width)
    wt_b = rows_wt.reshape(hot_count, blocks, capacity, slice_width)
    bg_b = back_gate_hot.reshape(hot_count, blocks, capacity, hidden_blk)
    bu_b = back_up_hot.reshape(hot_count, blocks, capacity, hidden_blk)
    hid_b = hidden_hot.reshape(hot_count, blocks, capacity, hidden_blk)
    blk_gate = jnp.einsum("jbcd,jbch->jbdh", feat_b, bg_b, preferred_element_type=jnp.float32)
    blk_up = jnp.einsum("jbcd,jbch->jbdh", feat_b, bu_b, preferred_element_type=jnp.float32)
    blk_down = jnp.einsum("jbch,jbcd->jbhd", hid_b, wt_b, preferred_element_type=jnp.float32)
    grad_gate_hot = jnp.sum(blk_gate.astype(jnp.bfloat16).astype(jnp.float32), axis=1)
    grad_up_hot = jnp.sum(blk_up.astype(jnp.bfloat16).astype(jnp.float32), axis=1)
    grad_down_hot = jnp.sum(blk_down.astype(jnp.bfloat16).astype(jnp.float32), axis=1)
    hot_route_all = lax.psum(hot_route_part, ("grp", "ep"))
    me = lax.axis_index("ep")
    hot_route = lax.dynamic_index_in_dim(
        hot_route_all.reshape(hot_count, blocks, capacity), me, axis=1, keepdims=False
    )
    cold_route = lax.psum(cold_route, "grp")
    cold_back = lax.all_to_all(
        cold_route.reshape(cold_count, capacity), "ep", split_axis=0, concat_axis=0, tiled=True
    )
    route_flat = jnp.dot(cold_back.reshape(-1), cold_map, precision=lax.Precision.HIGHEST)
    route_flat = route_flat + jnp.dot(
        hot_route.reshape(-1), hot_map, precision=lax.Precision.HIGHEST
    )
    gate_weight_grad = route_flat.reshape(tok_rows, top_count)
    return (
        grad_gate_cold[None].astype(jnp.bfloat16),
        grad_up_cold[None].astype(jnp.bfloat16),
        grad_down_cold[None].astype(jnp.bfloat16),
        grad_gate_hot,
        grad_up_hot,
        grad_down_hot,
        gate_weight_grad,
    )


def solution(mesh):
    in_specs = (
        P("ep", "grp"),
        P("ep", "grp"),
        P("ep", None),
        P("ep", None),
        P(),
        P("ep", "grp", None),
        P("ep", "grp", None),
        P("ep", None, "grp"),
        P(None, "grp", "ep"),
        P(None, "grp", "ep"),
        P(None, "ep", "grp"),
    )
    out_specs = (
        P("ep", "grp", None),
        P("ep", "grp", None),
        P("ep", None, "grp"),
        P(None, "grp", "ep"),
        P(None, "grp", "ep"),
        P(None, "ep", "grp"),
        P("ep", None),
    )
    return jax.shard_map(body, mesh=mesh, in_specs=in_specs, out_specs=out_specs, check_vma=False)
```

profile of v0, /device:TPU:0, one launch (start us, length us, event | category | flops | bytes accessed | tf_op | source)
XLA Modules:
  0.0 194.5 jit_solution(9976301442183095189)
XLA Ops:
  12.8 1.3 convolution_convert_fusion.8
  15.2 2.3 %reduce-window.14 = s32[8,12,128]{2,1,0:T(8,128)S(1)} reduce-window(s32[8,12,128]{2,1,0:T(8,128)S(1)} %fusion.69, s32[]{:T(128)} %constant.15.clone.1), window={size=1x1x128 pad=0_0x0_0x127_0}, to_apply=%region_1.2 | reduce-window | flops 1560576 | bytes 98308 | tf_op jit(solution)/shard_map/reduce-window
  19.1 7.3 %all-to-all-start.1 = ((bf16[8,1,16]{2,1,0:T(2,128)(2,1)}), bf16[8,1,16]{2,1,0:T(2,128)(2,1)S(1)}, u32[]{:S(2)}, u32[]{:S(2)}) async-start(bf16[8,1,16]{2,1,0:T(2,128)(2,1)} %all_to_all.24), calls=%async_computation.1 | async-start | bytes 8192 | tf_op jit(solution)/shard_map/all_to_all | solution.py:81
  28.0 4.8 %all-to-all-done.1 = bf16[8,1,16]{2,1,0:T(2,128)(2,1)S(1)} async-done(((bf16[8,1,16]{2,1,0:T(2,128)(2,1)}), bf16[8,1,16]{2,1,0:T(2,128)(2,1)S(1)}, u32[]{:S(2)}, u32[]{:S(2)}) %all-to-all-start.1) | async-done | bytes 288 | tf_op jit(solution)/shard_map/all_to_all | solution.py:81
  32.8 3.4 %all-to-all-start = ((bf16[8,16,1280]{2,1,0:T(8,128)(2,1)}), bf16[8,16,1280]{2,1,0:T(8,128)(2,1)S(1)}, u32[]{:S(2)}, u32[]{:S(2)}) async-start(bf16[8,16,1280]{2,1,0:T(8,128)(2,1)} %bitcast.165), calls=%async_computation | async-start | bytes 655360 | tf_op jit(solution)/shard_map/all_to_all | solution.py:79
  37.3 9.1 %all-to-all-done = bf16[8,16,1280]{2,1,0:T(8,128)(2,1)S(1)} async-done(((bf16[8,16,1280]{2,1,0:T(8,128)(2,1)}), bf16[8,16,1280]{2,1,0:T(8,128)(2,1)S(1)}, u32[]{:S(2)}, u32[]{:S(2)}) %all-to-all-start) | async-done | bytes 327712 | tf_op jit(solution)/shard_map/all_to_all | solution.py:79
  46.4 3.9 %all-to-all-start.2 = ((bf16[8,16,1280]{2,1,0:T(8,128)(2,1)}), bf16[8,16,1280]{2,1,0:T(8,128)(2,1)S(1)}, u32[]{:S(2)}, u32[]{:S(2)}) async-start(bf16[8,16,1280]{2,1,0:T(8,128)(2,1)} %bitcast.166), calls=%async_computation.2 | async-start | bytes 655360 | tf_op jit(solution)/shard_map/all_to_all | solution.py:80
  50.3 2.8 %fusion.20 = bf16[128,768]{1,0:T(8,128)(2,1)} fusion(bf16[128,1280]{1,0:T(8,128)(2,1)S(1)} %bitcast.155, bf16[1,1280,768]{2,1,0:T(8,128)(2,1)} %param.16), kind=kOutput, calls=%fused_computation.29 | convolution fusion | flops 251756544 | bytes 2490368 | tf_op jit(solution)/shard_map/dot_general | solution.py:91
  54.3 14.6 %all-to-all-done.2 = bf16[8,16,1280]{2,1,0:T(8,128)(2,1)S(1)} async-done(((bf16[8,16,1280]{2,1,0:T(8,128)(2,1)}), bf16[8,16,1280]{2,1,0:T(8,128)(2,1)S(1)}, u32[]{:S(2)}, u32[]{:S(2)}) %all-to-all-start.2) | async-done | bytes 327712 | tf_op jit(solution)/shard_map/all_to_all | solution.py:80
  69.0 1.5 fusion.14
  70.5 2.1 %all-gather.3.cloned.1.call-done = bf16[3,256,1280]{2,1,0:T(8,128)(2,1)} async-done(((bf16[3,32,1280]{2,1,0:T(8,128)(2,1)}), bf16[3,256,1280]{2,1,0:T(8,128)(2,1)}) %all-gather.3.cloned.1.call-update) | async-done | bytes 1966096 | tf_op jit(solution)/shard_map/all_gather | solution.py:119
  72.6 1.7 copy.68
  78.1 33.6 %all-reduce.3.cloned.1.call-done = (bf16[128,768]{1,0:T(8,128)(2,1)}, bf16[128,768]{1,0:T(8,128)(2,1)}, bf16[128,768]{1,0:T(8,128)(2,1)}, bf16[3,2,128,96]{2,3,1,0:T(8,128)(2,1)}) async-done(((bf16[128,768]{1,0:T(8,128)(2,1)}, bf16[128,768]{1,0:T(8,128)(2,1)}, bf16[128,768]{1,0:T(8,128)(2,1)}, bf16[3,2,128,96]{2,3,1,0:T(8,128)(2,1)}), (bf16[128,768]{1,0:T(8,128)(2,1)}, bf16[128,768]{1,0:T(8,128)(2,1)}, ...) | async-done | bytes 737296 | tf_op jit(solution)/shard_map/psum | solution.py:98
  111.7 1.6 convert_element_type.217
  114.5 3.3 %convert_reduce_fusion = f32[2,96,1280]{2,1,0:T(8,128)} fusion(f32[2,8,16,96]{3,2,1,0:T(8,128)S(1)} %bitcast.169, f32[2,8,16,96]{3,2,1,0:T(8,128)S(1)} %bitcast.171, bf16[3,2,8,16,1280]{4,3,2,1,0:T(8,128)(2,1)} %bitcast.152), kind=kOutput, calls=%fused_computation | convolution fusion | flops 68714496 | bytes 1835008 | tf_op jit(solution)/shard_map/jbch,jbcd->jbhd/dot_general | solution.py:146
  117.8 3.3 %convert_reduce_fusion.2 = f32[2,1280,96]{1,2,0:T(8,128)} fusion(f32[2,8,16,96]{3,2,1,0:T(8,128)S(1)} %bitcast.172, f32[2,8,16,96]{3,2,1,0:T(8,128)S(1)} %bitcast.174, f32[2,8,16,96]{3,2,1,0:T(8,128)S(1)} %bitcast.170, bf16[3,2,8,16,1280]{4,3,2,1,0:T(8,128)(2,1)} %bitcast.153), kind=kOutput, calls=%fused_computation.2 | convolution fusion | flops 68812800 | bytes 1933312 | tf_op jit(solution)/shard_map/jbcd,jbch->jbdh/dot_general | solution.py:144
  121.1 3.4 %convert_reduce_fusion.1 = f32[2,1280,96]{1,2,0:T(8,128)} fusion(f32[2,8,16,96]{3,2,1,0:T(8,128)S(1)} %bitcast.175, f32[2,8,16,96]{3,2,1,0:T(8,128)S(1)} %bitcast.173, bf16[3,2,8,16,1280]{4,3,2,1,0:T(8,128)(2,1)} %bitcast.154), kind=kOutput, calls=%fused_computation.1 | convolution fusion | flops 68714496 | bytes 1835008 | tf_op jit(solution)/shard_map/jbcd,jbch->jbdh/dot_general | solution.py:145
  124.6 2.0 %fusion.1 = bf16[1,1280,768]{2,1,0:T(8,128)(2,1)} fusion(bf16[128,1280]{1,0:T(8,128)(2,1)S(1)} %bitcast.157, bf16[128,768]{1,0:T(8,128)(2,1)S(1)} %copy-done.7, bf16[128,768]{1,0:T(8,128)(2,1)S(1)} %copy-done.5), kind=kOutput, calls=%fused_computation.10 | convolution fusion | flops 253427712 | bytes 2686976 | tf_op jit(solution)/shard_map/dot_general | solution.py:108
  126.5 2.0 %fusion = bf16[1,1280,768]{2,1,0:T(8,128)(2,1)} fusion(bf16[128,1280]{1,0:T(8,128)(2,1)S(1)} %bitcast.158, bf16[128,768]{1,0:T(8,128)(2,1)S(1)} %copy-done.6, bf16[128,768]{1,0:T(8,128)(2,1)S(1)} %copy-done.7, bf16[128,768]{1,0:T(8,128)(2,1)S(1)} %copy-done.5), kind=kOutput, calls=%fused_computation.9 | convolution fusion | flops 253919232 | bytes 2883584 | tf_op jit(solution)/shard_map/dot_general | solution.py:105
  129.2 6.2 %psum.46 = f32[8,1,16]{2,0,1:T(8,128)} all-reduce(f32[8,1,16]{2,0,1:T(8,128)S(1)} %all_to_all.22), channel_id=1, replica_groups=mesh['grp'=4,'ep'=8] {'grp'}, use_global_device_ids=true, to_apply=%region_20.21 | all-reduce | flops 128 | bytes 1024 | tf_op jit(solution)/shard_map/psum | solution.py:155
  135.4 5.5 %all-to-all-start.3 = ((f32[8,1,16]{2,1,0:T(1,128)}), f32[8,1,16]{2,1,0:T(1,128)S(1)}, u32[]{:S(2)}, u32[]{:S(2)}) async-start(f32[8,1,16]{2,1,0:T(1,128)} %bitcast.31), calls=%async_computation.3 | async-start | bytes 8192 | tf_op jit(solution)/shard_map/all_to_all | solution.py:156
  140.9 1.6 fusion.23
  142.6 40.2 %psum.47 = f32[2,8,16]{2,1,0:T(8,128)S(1)} all-reduce(f32[2,8,16]{2,1,0:T(8,128)S(1)} %reshape.204), channel_id=1, replica_groups=mesh['grp'=4,'ep'=8] {'grp','ep'}, use_global_device_ids=true, to_apply=%region_22.23 | all-reduce | flops 256 | bytes 2048 | tf_op jit(solution)/shard_map/psum | solution.py:150
  183.0 2.0 %fusion.2 = bf16[1,768,1280]{2,1,0:T(8,128)(2,1)} fusion(bf16[128,1280]{1,0:T(8,128)(2,1)S(1)} %fusion.37, bf16[128,768]{1,0:T(8,128)(2,1)S(1)} %copy-done.6, bf16[128,768]{1,0:T(8,128)(2,1)S(1)} %copy-done.5), kind=kOutput, calls=%fused_computation.11 | convolution fusion | flops 253427712 | bytes 2686976 | tf_op jit(solution)/shard_map/dot_general | solution.py:111
  (92 shorter events, 20.4 us)
Async XLA Ops:
  7.2 61.9 %copy-start = (bf16[1,768,1280]{2,1,0:T(8,128)(2,1)S(1)}, bf16[1,768,1280]{2,1,0:T(8,128)(2,1)}, u32[]{:S(2)}) copy-start(bf16[1,768,1280]{2,1,0:T(8,128)(2,1)} %param.18) | copy-start | bytes 5898244
  7.2 6.9 %copy-start.2 = (bf16[256,1280]{1,0:T(8,128)(2,1)S(1)}, bf16[256,1280]{1,0:T(8,128)(2,1)}, u32[]{:S(2)}) copy-start(bf16[256,1280]{1,0:T(8,128)(2,1)} %param.11) | copy-start | bytes 1966084
  7.2 65.4 %all-gather.3.cloned.1.call-start = ((), (), s32[]{:S(2)}) async-start(), calls=%async_computation.4 | async-start | bytes 2211840 | tf_op jit(solution)/shard_map/all_gather | solution.py:119
  14.4 21.8 %copy-start.3 = (bf16[256,1280]{1,0:T(8,128)(2,1)S(1)}, bf16[256,1280]{1,0:T(8,128)(2,1)}, u32[]{:S(2)}) copy-start(bf16[256,1280]{1,0:T(8,128)(2,1)} %param.12) | copy-start | bytes 1966084
  19.1 13.7 %all-to-all-start.1 = ((bf16[8,1,16]{2,1,0:T(2,128)(2,1)}), bf16[8,1,16]{2,1,0:T(2,128)(2,1)S(1)}, u32[]{:S(2)}, u32[]{:S(2)}) async-start(bf16[8,1,16]{2,1,0:T(2,128)(2,1)} %all_to_all.24), calls=%async_computation.1 | async-start | bytes 8192 | tf_op jit(solution)/shard_map/all_to_all | solution.py:81
  32.8 13.6 %all-to-all-start = ((bf16[8,16,1280]{2,1,0:T(8,128)(2,1)}), bf16[8,16,1280]{2,1,0:T(8,128)(2,1)S(1)}, u32[]{:S(2)}, u32[]{:S(2)}) async-start(bf16[8,16,1280]{2,1,0:T(8,128)(2,1)} %bitcast.165), calls=%async_computation | async-start | bytes 655360 | tf_op jit(solution)/shard_map/all_to_all | solution.py:79
  46.4 22.5 %all-to-all-start.2 = ((bf16[8,16,1280]{2,1,0:T(8,128)(2,1)}), bf16[8,16,1280]{2,1,0:T(8,128)(2,1)S(1)}, u32[]{:S(2)}, u32[]{:S(2)}) async-start(bf16[8,16,1280]{2,1,0:T(8,128)(2,1)} %bitcast.166), calls=%async_computation.2 | async-start | bytes 655360 | tf_op jit(solution)/shard_map/all_to_all | solution.py:80
  50.3 61.4 %all-reduce.3.cloned.1.call-start = ((), (), s32[]{:S(2)}) async-start(), calls=%async_computation.5 | async-start | bytes 1474560 | tf_op jit(solution)/shard_map/psum | solution.py:98
  50.3 2.8 %copy-start.4 = (bf16[1,1280,768]{2,1,0:T(8,128)(2,1)S(1)}, bf16[1,1280,768]{2,1,0:T(8,128)(2,1)}, u32[]{:S(2)}) copy-start(bf16[1,1280,768]{2,1,0:T(8,128)(2,1)} %param.17) | copy-start | bytes 5898244
  74.3 1.5 copy-start.1
  74.3 1.5 copy-start.8
  74.4 1.9 copy-start.9
  75.8 1.1 copy-start.10
  121.1 3.4 %copy-start.5 = (bf16[128,768]{1,0:T(8,128)(2,1)S(1)}, bf16[128,768]{1,0:T(8,128)(2,1)}, u32[]{:S(2)}) copy-start(bf16[128,768]{1,0:T(8,128)(2,1)} %get-tuple-element.36) | copy-start | bytes 589828
  121.1 3.4 %copy-start.7 = (bf16[128,768]{1,0:T(8,128)(2,1)S(1)}, bf16[128,768]{1,0:T(8,128)(2,1)}, u32[]{:S(2)}) copy-start(bf16[128,768]{1,0:T(8,128)(2,1)} %get-tuple-element.35) | copy-start | bytes 589828
  124.5 2.0 %copy-start.6 = (bf16[128,768]{1,0:T(8,128)(2,1)S(1)}, bf16[128,768]{1,0:T(8,128)(2,1)}, u32[]{:S(2)}) copy-start(bf16[128,768]{1,0:T(8,128)(2,1)} %get-tuple-element.34) | copy-start | bytes 589828
  135.4 49.7 %all-to-all-start.3 = ((f32[8,1,16]{2,1,0:T(1,128)}), f32[8,1,16]{2,1,0:T(1,128)S(1)}, u32[]{:S(2)}, u32[]{:S(2)}) async-start(f32[8,1,16]{2,1,0:T(1,128)} %bitcast.31), calls=%async_computation.3 | async-start | bytes 8192 | tf_op jit(solution)/shard_map/all_to_all | solution.py:156
Sparse Core Ops, SparseCore 0:
  15.3 57.2 all-gather.2
  78.1 33.5 all-reduce.2
where the time goes:
time: 195 us
  waiting for transfers between devices  64.2 us (33%)
  blocking collectives  46.4 us (24%)
  matrix products  29.2 us (15%)
  starting transfers between devices  20.2 us (10%)
  between operations  14.4 us (7%)
  local copies, waits for them, and re-layouts  10.9 us (6%)
  other arithmetic  9.22 us (5%)
    psum x1, blocking collectives, body(): hot_route_all = lax.psum(hot_route_part, ('grp', 'ep'))  40.2 us
    psum x1, waiting for transfers between devices, body(): lax.psum(part_up.astype(jnp.bfloat16), 'grp').astype(jnp.float32)  33.6 us
    all_to_all x1, waiting for transfers between devices, body(): lax.all_to_all(outgoing[1], 'ep', split_axis=0, concat_axis=0, tiled=True)  14.6 us
    all_to_all x1, waiting for transfers between devices, body(): lax.all_to_all(outgoing[0], 'ep', split_axis=0, concat_axis=0, tiled=True)  9.11 us
    all_to_all x1, starting transfers between devices, body(): lax.all_to_all(outgoing[2], 'ep', split_axis=0, concat_axis=0, tiled=True)  7.28 us
    psum x1, blocking collectives, body(): cold_route = lax.psum(cold_route, 'grp')  6.24 us
    all_to_all x1, starting transfers between devices, body(): lax.all_to_all(cold_route.reshape(cold_count, capacity), 'ep', split_axis...  5.52 us
    all_to_all x1, waiting for transfers between devices, body(): lax.all_to_all(outgoing[2], 'ep', split_axis=0, concat_axis=0, tiled=True)  4.77 us
  transfers between devices with their start and end apart: 6, of which 5 were waited for; matrix products, arithmetic and copies ran while one was open for 8% of the time, Pallas kernels for 0%

commit v1 on v0

--- a/solution.py
+++ b/solution.py
@@ -147,7 +147,7 @@
     grad_gate_hot = jnp.sum(blk_gate.astype(jnp.bfloat16).astype(jnp.float32), axis=1)
     grad_up_hot = jnp.sum(blk_up.astype(jnp.bfloat16).astype(jnp.float32), axis=1)
     grad_down_hot = jnp.sum(blk_down.astype(jnp.bfloat16).astype(jnp.float32), axis=1)
-    hot_route_all = lax.psum(hot_route_part, ("grp", "ep"))
+    hot_route_all = jnp.sum(lax.all_gather(hot_route_part, ("grp", "ep")), axis=0)
     me = lax.axis_index("ep")
     hot_route = lax.dynamic_index_in_dim(
         hot_route_all.reshape(hot_count, blocks, capacity), me, axis=1, keepdims=False

time: 195 us -> 223 us (1.14)
  blocking collectives: 46.4 us -> 73.6 us
    all_gather x0 -> x1, blocking collectives: none -> 67.3 us  [body(): lax.all_gather(hot_route_part, ('grp', 'ep'))]
    psum x1 -> x0, blocking collectives: 40.2 us -> none  [body(): hot_route_all = lax.psum(hot_route_part, ('grp', 'ep'))]
  transfers between devices with their start and end apart: 6 -> 6, of which waited for: 5 -> 5; matrix products, arithmetic and copies ran while one was open for 8% -> 7% of each run, Pallas kernels for 0% -> 0%
where the time goes in v1:
time: 223 us; the launch traced here: 222 us
  blocking collectives  73.6 us (33%)
  waiting for transfers between devices  64.2 us (29%)
  matrix products  29.2 us (13%)
  starting transfers between devices  20.2 us (9%)
  between operations  14.4 us (6%)
  local copies, waits for them, and re-layouts  10.9 us (5%)
  other arithmetic  9.26 us (4%)
    all_gather x1, blocking collectives, body(): lax.all_gather(hot_route_part, ('grp', 'ep'))  67.3 us
    psum x1, waiting for transfers between devices, body(): lax.psum(part_up.astype(jnp.bfloat16), 'grp').astype(jnp.float32)  33.6 us
    all_to_all x1, waiting for transfers between devices, body(): lax.all_to_all(outgoing[1], 'ep', split_axis=0, concat_axis=0, tiled=True)  14.6 us
    all_to_all x1, waiting for transfers between devices, body(): lax.all_to_all(outgoing[0], 'ep', split_axis=0, concat_axis=0, tiled=True)  9.11 us
    all_to_all x1, starting transfers between devices, body(): lax.all_to_all(outgoing[2], 'ep', split_axis=0, concat_axis=0, tiled=True)  7.28 us
    psum x1, blocking collectives, body(): cold_route = lax.psum(cold_route, 'grp')  6.24 us
    all_to_all x1, starting transfers between devices, body(): lax.all_to_all(cold_route.reshape(cold_count, capacity), 'ep', split_axis...  5.52 us
    all_to_all x1, waiting for transfers between devices, body(): lax.all_to_all(outgoing[2], 'ep', split_axis=0, concat_axis=0, tiled=True)  4.77 us
  transfers between devices with their start and end apart: 6, of which 5 were waited for; matrix products, arithmetic and copies ran while one was open for 7% of the time, Pallas kernels for 0%

profile of v1, /device:TPU:0, one launch (start us, length us, event | category | flops | bytes accessed | tf_op | source)
XLA Modules:
  0.0 221.7 jit_solution(12911008587821388085)
XLA Ops:
  12.8 1.3 convolution_convert_fusion.8
  15.2 2.3 %reduce-window.14 = s32[8,12,128]{2,1,0:T(8,128)S(1)} reduce-window(s32[8,12,128]{2,1,0:T(8,128)S(1)} %fusion.69, s32[]{:T(128)} %constant.15.clone.1), window={size=1x1x128 pad=0_0x0_0x127_0}, to_apply=%region_1.2 | reduce-window | flops 1560576 | bytes 98308 | tf_op jit(solution)/shard_map/reduce-window
  19.1 7.3 %all-to-all-start.1 = ((bf16[8,1,16]{2,1,0:T(2,128)(2,1)}), bf16[8,1,16]{2,1,0:T(2,128)(2,1)S(1)}, u32[]{:S(2)}, u32[]{:S(2)}) async-start(bf16[8,1,16]{2,1,0:T(2,128)(2,1)} %all_to_all.24), calls=%async_computation.1 | async-start | bytes 8192 | tf_op jit(solution)/shard_map/all_to_all | solution.py:81
  28.0 4.8 %all-to-all-done.1 = bf16[8,1,16]{2,1,0:T(2,128)(2,1)S(1)} async-done(((bf16[8,1,16]{2,1,0:T(2,128)(2,1)}), bf16[8,1,16]{2,1,0:T(2,128)(2,1)S(1)}, u32[]{:S(2)}, u32[]{:S(2)}) %all-to-all-start.1) | async-done | bytes 288 | tf_op jit(solution)/shard_map/all_to_all | solution.py:81
  32.8 3.4 %all-to-all-start = ((bf16[8,16,1280]{2,1,0:T(8,128)(2,1)}), bf16[8,16,1280]{2,1,0:T(8,128)(2,1)S(1)}, u32[]{:S(2)}, u32[]{:S(2)}) async-start(bf16[8,16,1280]{2,1,0:T(8,128)(2,1)} %bitcast.166), calls=%async_computation | async-start | bytes 655360 | tf_op jit(solution)/shard_map/all_to_all | solution.py:79
  37.3 9.1 %all-to-all-done = bf16[8,16,1280]{2,1,0:T(8,128)(2,1)S(1)} async-done(((bf16[8,16,1280]{2,1,0:T(8,128)(2,1)}), bf16[8,16,1280]{2,1,0:T(8,128)(2,1)S(1)}, u32[]{:S(2)}, u32[]{:S(2)}) %all-to-all-start) | async-done | bytes 327712 | tf_op jit(solution)/shard_map/all_to_all | solution.py:79
  46.4 3.9 %all-to-all-start.2 = ((bf16[8,16,1280]{2,1,0:T(8,128)(2,1)}), bf16[8,16,1280]{2,1,0:T(8,128)(2,1)S(1)}, u32[]{:S(2)}, u32[]{:S(2)}) async-start(bf16[8,16,1280]{2,1,0:T(8,128)(2,1)} %bitcast.167), calls=%async_computation.2 | async-start | bytes 655360 | tf_op jit(solution)/shard_map/all_to_all | solution.py:80
  50.3 2.8 %fusion.20 = bf16[128,768]{1,0:T(8,128)(2,1)} fusion(bf16[128,1280]{1,0:T(8,128)(2,1)S(1)} %bitcast.156, bf16[1,1280,768]{2,1,0:T(8,128)(2,1)} %param.16), kind=kOutput, calls=%fused_computation.29 | convolution fusion | flops 251756544 | bytes 2490368 | tf_op jit(solution)/shard_map/dot_general | solution.py:91
  54.3 14.6 %all-to-all-done.2 = bf16[8,16,1280]{2,1,0:T(8,128)(2,1)S(1)} async-done(((bf16[8,16,1280]{2,1,0:T(8,128)(2,1)}), bf16[8,16,1280]{2,1,0:T(8,128)(2,1)S(1)}, u32[]{:S(2)}, u32[]{:S(2)}) %all-to-all-start.2) | async-done | bytes 327712 | tf_op jit(solution)/shard_map/all_to_all | solution.py:80
  69.0 1.5 fusion.14
  70.5 2.1 all-gather.5.cloned.1.call-done
  72.6 1.7 copy.68
  78.1 33.6 %all-reduce.3.cloned.1.call-done = (bf16[128,768]{1,0:T(8,128)(2,1)}, bf16[128,768]{1,0:T(8,128)(2,1)}, bf16[128,768]{1,0:T(8,128)(2,1)}, bf16[3,2,128,96]{2,3,1,0:T(8,128)(2,1)}) async-done(((bf16[128,768]{1,0:T(8,128)(2,1)}, bf16[128,768]{1,0:T(8,128)(2,1)}, bf16[128,768]{1,0:T(8,128)(2,1)}, bf16[3,2,128,96]{2,3,1,0:T(8,128)(2,1)}), (bf16[128,768]{1,0:T(8,128)(2,1)}, bf16[128,768]{1,0:T(8,128)(2,1)}, ...) | async-done | bytes 737296 | tf_op jit(solution)/shard_map/psum | solution.py:98
  111.7 1.6 convert_element_type.217
  114.5 3.3 %convert_reduce_fusion = f32[2,96,1280]{2,1,0:T(8,128)} fusion(f32[2,8,16,96]{3,2,1,0:T(8,128)S(1)} %bitcast.170, f32[2,8,16,96]{3,2,1,0:T(8,128)S(1)} %bitcast.172, bf16[3,2,8,16,1280]{4,3,2,1,0:T(8,128)(2,1)} %bitcast.153), kind=kOutput, calls=%fused_computation | convolution fusion | flops 68714496 | bytes 1835008 | tf_op jit(solution)/shard_map/jbch,jbcd->jbhd/dot_general | solution.py:146
  117.8 3.3 %convert_reduce_fusion.2 = f32[2,1280,96]{1,2,0:T(8,128)} fusion(f32[2,8,16,96]{3,2,1,0:T(8,128)S(1)} %bitcast.173, f32[2,8,16,96]{3,2,1,0:T(8,128)S(1)} %bitcast.175, f32[2,8,16,96]{3,2,1,0:T(8,128)S(1)} %bitcast.171, bf16[3,2,8,16,1280]{4,3,2,1,0:T(8,128)(2,1)} %bitcast.154), kind=kOutput, calls=%fused_computation.2 | convolution fusion | flops 68812800 | bytes 1933312 | tf_op jit(solution)/shard_map/jbcd,jbch->jbdh/dot_general | solution.py:144
  121.1 3.4 %convert_reduce_fusion.1 = f32[2,1280,96]{1,2,0:T(8,128)} fusion(f32[2,8,16,96]{3,2,1,0:T(8,128)S(1)} %bitcast.176, f32[2,8,16,96]{3,2,1,0:T(8,128)S(1)} %bitcast.174, bf16[3,2,8,16,1280]{4,3,2,1,0:T(8,128)(2,1)} %bitcast.155), kind=kOutput, calls=%fused_computation.1 | convolution fusion | flops 68714496 | bytes 1835008 | tf_op jit(solution)/shard_map/jbcd,jbch->jbdh/dot_general | solution.py:145
  124.6 2.0 fusion.1
  126.5 2.0 fusion
  129.2 6.2 %psum.39 = f32[8,1,16]{2,0,1:T(8,128)} all-reduce(f32[8,1,16]{2,0,1:T(8,128)S(1)} %all_to_all.22), channel_id=1, replica_groups=mesh['grp'=4,'ep'=8] {'grp'}, use_global_device_ids=true, to_apply=%region_20.21 | all-reduce | flops 128 | bytes 1024 | tf_op jit(solution)/shard_map/psum | solution.py:155
  135.4 5.5 %all-to-all-start.3 = ((f32[8,1,16]{2,1,0:T(1,128)}), f32[8,1,16]{2,1,0:T(1,128)S(1)}, u32[]{:S(2)}, u32[]{:S(2)}) async-start(f32[8,1,16]{2,1,0:T(1,128)} %bitcast.31), calls=%async_computation.3 | async-start | bytes 8192 | tf_op jit(solution)/shard_map/all_to_all | solution.py:156
  140.9 1.6 fusion.23
  142.6 67.3 %all-gather.2 = f32[32,2,128]{2,1,0:T(2,128)S(1)} all-gather(f32[1,2,128]{2,1,0:T(2,128)S(1)} %bitcast.179), channel_id=3, replica_groups=mesh['grp'=4,'ep'=8] {'grp','ep'}, dimensions={0}, use_global_device_ids=true | all-gather | bytes 33792 | tf_op jit(solution)/shard_map/all_gather | solution.py:150
  210.1 2.0 fusion.2
  (93 shorter events, 20.5 us)
Async XLA Ops:
  7.2 61.9 %copy-start = (bf16[1,768,1280]{2,1,0:T(8,128)(2,1)S(1)}, bf16[1,768,1280]{2,1,0:T(8,128)(2,1)}, u32[]{:S(2)}) copy-start(bf16[1,768,1280]{2,1,0:T(8,128)(2,1)} %param.18) | copy-start | bytes 5898244
  7.2 6.9 %copy-start.2 = (bf16[256,1280]{1,0:T(8,128)(2,1)S(1)}, bf16[256,1280]{1,0:T(8,128)(2,1)}, u32[]{:S(2)}) copy-start(bf16[256,1280]{1,0:T(8,128)(2,1)} %param.11) | copy-start | bytes 1966084
  7.2 65.4 %all-gather.5.cloned.1.call-start = ((), (), s32[]{:S(2)}) async-start(), calls=%async_computation.4 | async-start | bytes 2211840 | tf_op jit(solution)/shard_map/all_gather | solution.py:119
  14.4 21.8 %copy-start.3 = (bf16[256,1280]{1,0:T(8,128)(2,1)S(1)}, bf16[256,1280]{1,0:T(8,128)(2,1)}, u32[]{:S(2)}) copy-start(bf16[256,1280]{1,0:T(8,128)(2,1)} %param.12) | copy-start | bytes 1966084
  19.1 13.7 %all-to-all-start.1 = ((bf16[8,1,16]{2,1,0:T(2,128)(2,1)}), bf16[8,1,16]{2,1,0:T(2,128)(2,1)S(1)}, u32[]{:S(2)}, u32[]{:S(2)}) async-start(bf16[8,1,16]{2,1,0:T(2,128)(2,1)} %all_to_all.24), calls=%async_computation.1 | async-start | bytes 8192 | tf_op jit(solution)/shard_map/all_to_all | solution.py:81
  32.8 13.6 %all-to-all-start = ((bf16[8,16,1280]{2,1,0:T(8,128)(2,1)}), bf16[8,16,1280]{2,1,0:T(8,128)(2,1)S(1)}, u32[]{:S(2)}, u32[]{:S(2)}) async-start(bf16[8,16,1280]{2,1,0:T(8,128)(2,1)} %bitcast.166), calls=%async_computation | async-start | bytes 655360 | tf_op jit(solution)/shard_map/all_to_all | solution.py:79
  46.4 22.5 %all-to-all-start.2 = ((bf16[8,16,1280]{2,1,0:T(8,128)(2,1)}), bf16[8,16,1280]{2,1,0:T(8,128)(2,1)S(1)}, u32[]{:S(2)}, u32[]{:S(2)}) async-start(bf16[8,16,1280]{2,1,0:T(8,128)(2,1)} %bitcast.167), calls=%async_computation.2 | async-start | bytes 655360 | tf_op jit(solution)/shard_map/all_to_all | solution.py:80
  50.3 61.4 %all-reduce.3.cloned.1.call-start = ((), (), s32[]{:S(2)}) async-start(), calls=%async_computation.5 | async-start | bytes 1474560 | tf_op jit(solution)/shard_map/psum | solution.py:98
  50.3 2.8 %copy-start.4 = (bf16[1,1280,768]{2,1,0:T(8,128)(2,1)S(1)}, bf16[1,1280,768]{2,1,0:T(8,128)(2,1)}, u32[]{:S(2)}) copy-start(bf16[1,1280,768]{2,1,0:T(8,128)(2,1)} %param.17) | copy-start | bytes 5898244
  74.3 1.5 copy-start.1
  74.3 1.5 copy-start.8
  74.4 1.9 copy-start.9
  75.8 1.1 copy-start.10
  121.1 3.4 %copy-start.5 = (bf16[128,768]{1,0:T(8,128)(2,1)S(1)}, bf16[128,768]{1,0:T(8,128)(2,1)}, u32[]{:S(2)}) copy-start(bf16[128,768]{1,0:T(8,128)(2,1)} %get-tuple-element.36) | copy-start | bytes 589828
  121.1 3.4 %copy-start.7 = (bf16[128,768]{1,0:T(8,128)(2,1)S(1)}, bf16[128,768]{1,0:T(8,128)(2,1)}, u32[]{:S(2)}) copy-start(bf16[128,768]{1,0:T(8,128)(2,1)} %get-tuple-element.35) | copy-start | bytes 589828
  124.5 2.0 copy-start.6
  135.4 76.9 %all-to-all-start.3 = ((f32[8,1,16]{2,1,0:T(1,128)}), f32[8,1,16]{2,1,0:T(1,128)S(1)}, u32[]{:S(2)}, u32[]{:S(2)}) async-start(f32[8,1,16]{2,1,0:T(1,128)} %bitcast.31), calls=%async_computation.3 | async-start | bytes 8192 | tf_op jit(solution)/shard_map/all_to_all | solution.py:156
Sparse Core Ops, SparseCore 0:
  15.3 57.2 all-gather.4
  78.1 33.5 all-reduce.2
